TPU v7x, 128 devices: a whole 4x4x4 slice. The times are simulated.
128 devices in a mesh: req: 16 (over y, z), mp: 8 (over x, core).
Axes of the slice: x: 4, y: 4, z: 4, core: 2. Of those that a mesh axis runs over, the one named last changes fastest.
Arguments:
- hidden_in: bfloat16 [16384, 2048], P('req', 'mp'), may hold values from -6 to 6
- w_qkv: bfloat16 [3, 2048, 2048], P(None, 'req', 'mp'), may hold values from -0.125 to 0.125
- w_out: bfloat16 [2048, 2048], P('mp', 'req'), may hold values from -0.125 to 0.125
- attn_gain: bfloat16 [2048], replicated, may hold values from 0.099609375 to 1.8984375
- mlp_gain: bfloat16 [2048], replicated, may hold values from 0.099609375 to 1.8984375
- w_gate: bfloat16 [2048, 8192], P('req', 'mp'), may hold values from -0.125 to 0.125
- w_up: bfloat16 [2048, 8192], P('req', 'mp'), may hold values from -0.125 to 0.125
- w_down: bfloat16 [8192, 2048], P('mp', 'req'), may hold values from -0.0625 to 0.0625
- k_cache: bfloat16 [16, 4096, 2048], P('req', None, 'mp'), may hold values from -363 to 363
- v_cache: bfloat16 [16, 4096, 2048], P('req', None, 'mp'), may hold values from -6 to 6
- cache_len: int32 [16], P('req'), may hold values from 256 to 4096, as said below
Outputs:
- hidden_out: bfloat16 [16384, 2048], P('req', 'mp')
- new_keys: bfloat16 [16384, 2048], P('req', 'mp')
- new_values: bfloat16 [16384, 2048], P('req', 'mp')
Inputs may be any that keep to these rules, and one draw needn't show every extreme that they name: Each request uses its first cache_len slots; later slots hold unused data. Some request's cache is full in every draw.
All inputs are finite; a program needn't handle non-finite values.
Results may differ from a plain program's by a relative error of at most 0.02.
Values may be sent and summed in bfloat16 or wider, within the bound.
No kernel may reach another device: no remote copies, remote signals or barrier semaphores. Data moves between devices by JAX's collectives and lax.ppermute only.
A program may use at most 128 MiB of HBM per device.

v0:
```python
import jax
import jax.numpy as jnp
from jax import lax
from jax.sharding import PartitionSpec as P

HD = 64
THETA = 130000.0
EPSILON = 1e-05
NEG_FILL = -1e30


def rms_scale(rows, gain):
    values = rows.astype(jnp.float32)
    meansq = jnp.mean(values * values, axis=-1, keepdims=True)
    return (values * lax.rsqrt(meansq + EPSILON) * gain.astype(jnp.float32)).astype(jnp.bfloat16)


def rotate(tensor, positions):
    half = tensor.shape[-1] // 2
    freq = THETA ** (-(jnp.arange(half, dtype=jnp.float32) * 2.0 / tensor.shape[-1]))
    angle = positions[:, None, None] * freq[None, None, :]
    cosine = jnp.cos(angle)
    sine = jnp.sin(angle)
    first = tensor[..., :half]
    second = tensor[..., half:]
    return jnp.concatenate(
        [first * cosine - second * sine, second * cosine + first * sine], axis=-1
    )


def absorb(carry, queries, keys, values, valid):
    top, total, accum = carry
    scores = jnp.einsum("qhd,khd->hqk", queries, keys, preferred_element_type=jnp.float32) * HD ** (
        -0.5
    )
    scores = jnp.where(valid[None], scores, NEG_FILL)
    new_top = jnp.maximum(top, jnp.max(scores, axis=-1, keepdims=True))
    factor = jnp.exp(top - new_top)
    probs = jnp.where(valid[None], jnp.exp(scores - new_top), 0.0)
    total = total * factor + jnp.sum(probs, axis=-1, keepdims=True)
    accum = accum * factor + jnp.einsum(
        "hqk,khd->hqd", probs.astype(jnp.bfloat16), values, preferred_element_type=jnp.float32
    )
    return (new_top, total, accum)


def on_device(
    hidden_in, w_qkv, w_out, attn_gain, mlp_gain, w_gate, w_up, w_down, k_cache, v_cache, cache_len
):
    new_count = hidden_in.shape[0]
    width = w_qkv.shape[2]
    heads_local = width // HD
    slots = k_cache.shape[1]
    full_rows = lax.all_gather(hidden_in, "mp", axis=1, tiled=True)
    normed = rms_scale(full_rows, attn_gain)
    columns = normed
    projected = jnp.einsum(
        "nd,kdw->knw",
        columns,
        lax.all_gather(w_qkv, "req", axis=1, tiled=True),
        preferred_element_type=jnp.float32,
    )
    length = cache_len[0]
    positions = (length + jnp.arange(new_count, dtype=jnp.int32)).astype(jnp.float32)
    queries = rotate(projected[0].reshape(new_count, heads_local, HD), positions).astype(
        jnp.bfloat16
    )
    fresh_keys = rotate(projected[1].reshape(new_count, heads_local, HD), positions).astype(
        jnp.bfloat16
    )
    fresh_values = projected[2].astype(jnp.bfloat16).reshape(new_count, heads_local, HD)
    rows = jnp.arange(new_count, dtype=jnp.int32)
    causal = rows[:, None] >= rows[None, :]
    start_carry = (
        jnp.full((heads_local, new_count, 1), NEG_FILL, jnp.float32),
        jnp.zeros((heads_local, new_count, 1), jnp.float32),
        jnp.zeros((heads_local, new_count, HD), jnp.float32),
    )
    carry = absorb(start_carry, queries, fresh_keys, fresh_values, causal)
    cache_keys = k_cache[0].reshape(slots, heads_local, HD)
    cache_values = v_cache[0].reshape(slots, heads_local, HD)
    block = min(slots, 512)
    count = (length + block - 1) // block

    def step_block(index, state):
        begin = index * block
        keys = lax.dynamic_slice_in_dim(cache_keys, begin, block, 0)
        values = lax.dynamic_slice_in_dim(cache_values, begin, block, 0)
        valid = (begin + jnp.arange(block, dtype=jnp.int32) < length)[None, :]
        return absorb(state, queries, keys, values, valid)

    top, total, accum = lax.fori_loop(0, count, step_block, carry)
    attn = (accum / total).transpose(1, 0, 2).reshape(new_count, width).astype(jnp.bfloat16)
    partial_value = jnp.dot(
        attn, lax.all_gather(w_out, "req", axis=1, tiled=True), preferred_element_type=jnp.float32
    )
    summed = lax.psum_scatter(
        partial_value.astype(jnp.bfloat16), "mp", scatter_dimension=1, tiled=True
    ).astype(jnp.float32)
    mid_local = (hidden_in.astype(jnp.float32) + summed).astype(jnp.bfloat16)
    mid_full = lax.all_gather(mid_local, "mp", axis=1, tiled=True)
    normed2 = rms_scale(mid_full, mlp_gain)
    columns = normed2
    gate = jnp.dot(
        columns,
        lax.all_gather(w_gate, "req", axis=0, tiled=True),
        preferred_element_type=jnp.float32,
    )
    upper = jnp.dot(
        columns, lax.all_gather(w_up, "req", axis=0, tiled=True), preferred_element_type=jnp.float32
    )
    units = (jax.nn.silu(gate) * upper).astype(jnp.bfloat16)
    terms = jnp.dot(
        units, lax.all_gather(w_down, "req", axis=1, tiled=True), preferred_element_type=jnp.float32
    )
    reduced = lax.psum_scatter(
        terms.astype(jnp.bfloat16), "mp", scatter_dimension=1, tiled=True
    ).astype(jnp.float32)
    hidden_out = (mid_local.astype(jnp.float32) + reduced).astype(jnp.bfloat16)
    return (
        hidden_out,
        fresh_keys.reshape(new_count, width),
        fresh_values.reshape(new_count, width),
    )


def solution(mesh):
    return jax.shard_map(
        on_device,
        mesh=mesh,
        in_specs=(
            P("req", "mp"),
            P(None, "req", "mp"),
            P("mp", "req"),
            P(),
            P(),
            P("req", "mp"),
            P("req", "mp"),
            P("mp", "req"),
            P("req", None, "mp"),
            P("req", None, "mp"),
            P("req"),
        ),
        out_specs=(P("req", "mp"), P("req", "mp"), P("req", "mp")),
        check_vma=False,
    )
```

profile of v0, /device:TPU:0, one launch (start us, length us, event | category | flops | bytes accessed | tf_op | source)
XLA Modules:
  0.0 499.0 jit_solution(9587442802145398446)
XLA Ops:
  7.2 0.0 all-gather.8.cloned.1.call-start
  7.2 0.7 all-gather.8.cloned.1.call-update
  7.9 0.0 all-gather.10.cloned.1.call-start
  7.9 1.7 copy.15
  9.7 0.0 all-gather.10.cloned.1.call-update
  9.7 0.0 all-gather.12.cloned.1.call-start
  9.8 0.7 all-gather.12.cloned.1.call-update
  10.4 0.0 reduce-scatter.3.cloned.1.call-start
  10.5 1.3 iota_compare_fusion
  12.4 0.7 convert_element_type.87
  13.1 2.9 copy.17
  16.1 4.2 copy.18
  20.2 0.5 multiply_cosine_fusion
  20.8 27.4 %all-gather.8.cloned.1.call-done = bf16[1024,2048]{1,0:T(8,128)(2,1)} async-done(((bf16[1024,256]{1,0:T(8,128)(2,1)}), bf16[1024,2048]{1,0:T(8,128)(2,1)}) %all-gather.8.cloned.1.call-update) | async-done | bytes 4194320 | tf_op jit(solution)/shard_map/all_gather | solution.py:54
  48.2 3.1 fusion.23
  51.3 53.4 %all-gather.10.cloned.1.call-done = bf16[3,2048,256]{1,2,0:T(8,128)(2,1)} async-done(((bf16[3,128,256]{1,2,0:T(8,128)(2,1)}), bf16[3,2048,256]{1,2,0:T(8,128)(2,1)}) %all-gather.10.cloned.1.call-update) | async-done | bytes 3145744 | tf_op jit(solution)/shard_map/all_gather | solution.py:60
  104.7 6.6 %fusion.37 = f32[3,1024,256]{1,2,0:T(8,128)S(1)} fusion(bf16[3,2048,256]{1,2,0:T(8,128)(2,1)} %all-gather.10.cloned.1.call-done, bf16[1024,2048]{1,0:T(8,128)(2,1)} %all-gather.8.cloned.1.call-done, f32[2048]{0:T(1024)S(1)} %convert_element_type.87, f32[1024]{0:T(1024)S(1)} %add_rsqrt_fusion.1), kind=kOutput, calls=%fused_computation.49 | convolution fusion | flops 3229614080 | bytes 10498048 | tf_op jit(solution)/shard_map/nd,kdw->knw/dot_general | solution.py:57
  111.3 0.0 copy-start.2
  111.3 0.0 copy-start.1
  111.3 0.2 fusion.54
  111.6 0.1 slice.44
  111.6 0.2 subtract_convert_fusion
  111.8 0.2 multiply_subtract_fusion
  112.0 1.0 copy-done.2
  113.0 0.3 copy-done.1
  113.3 3.0 fusion.20
  116.4 4.2 fusion.22
  120.6 5.9 %fusion.40 = f32[4,1024,64]{1,2,0:T(8,128)} fusion(bf16[1024,4,64]{0,2,1:T(8,128)(2,1)S(1)} %bitcast.80, f32[4,1024,1024]{1,2,0:T(8,128)S(1)} %get-tuple-element.91, f32[4,1024]{1,0:T(4,128)S(1)} %get-tuple-element.87, pred[1024,1024]{0,1:T(8,128)(4,1)S(1)} %copy-done.1, f32[4,1024]{1,0:T(4,128)S(1)} %get-tuple-element.85), kind=kOutput, calls=%fused_computation.50 | convolution fusion | flops 558104576 | bytes 19431424 | tf_op jit(solution)/shard_map/hqk,khd->hqd/dot_general | solution.py:41
  126.5 8.1 %while.14 = (s32[]{:T(128)}, f32[4,1024,1]{1,0,2:T(4,128)S(1)}, f32[4,1024,1]{1,0,2:T(4,128)S(1)}, f32[4,1024,64]{1,2,0:T(8,128)}, s32[]{:T(128)}, /*index=5*/s3...) while((s32[]{:T(128)}, f32[4,1024,1]{1,0,2:T(4,128)S(1)}, ...), condition=%wide.region_6.7_spmd, body=%wide.region_3.6_spmd.sunk | while | flops 564671488 | bytes 36965104 | solution.py:92
  126.5 0.7 add_compare_fusion.2
  127.3 1.6 bitcast_reduce_fusion.2
  128.9 3.1 fusion.74
  132.0 0.0 copy-start.5
  132.0 2.5 fusion.73
  134.6 0.0 copy-start.3
  134.6 0.0 copy-start.6
  134.6 1.4 divide_convert_fusion
  136.0 13.5 %all-gather.12.cloned.1.call-done = bf16[256,2048]{1,0:T(8,128)(2,1)} async-done(((bf16[256,128]{1,0:T(8,128)(2,1)}), bf16[256,2048]{1,0:T(8,128)(2,1)}) %all-gather.12.cloned.1.call-update) | async-done | bytes 1048592 | tf_op jit(solution)/shard_map/all_gather | solution.py:95
  149.5 4.5 convolution_convert_fusion
  154.0 0.0 reduce-scatter.3.cloned.1.call-update
  154.0 0.0 all-gather.14.cloned.1.call-start
  154.1 79.0 %reduce-scatter.3.cloned.1.call-done = bf16[1024,256]{1,0:T(8,128)(2,1)} async-done(((bf16[1024,2048]{1,0:T(8,128)(2,1)}), bf16[1024,256]{1,0:T(8,128)(2,1)}) %reduce-scatter.3.cloned.1.call-update) | async-done | bytes 524304 | tf_op jit(solution)/shard_map/reduce_scatter | solution.py:97
  233.1 2.0 add_convert_fusion.1
  235.1 0.0 all-gather.14.cloned.1.call-update
  235.1 0.0 all-gather.16.cloned.1.call-start
  235.2 0.5 all-gather.16.cloned.1.call-update
  235.7 0.0 all-gather.18.cloned.1.call-start
  235.7 0.7 all-gather.18.cloned.1.call-update
  236.4 0.0 all-gather.20.cloned.1.call-start
  236.5 0.7 all-gather.20.cloned.1.call-update
  237.2 0.3 reduce-scatter.5.cloned.1.call-start
  237.5 32.8 %all-gather.14.cloned.1.call-done = bf16[1024,2048]{1,0:T(8,128)(2,1)} async-done(((bf16[1024,256]{1,0:T(8,128)(2,1)}), bf16[1024,2048]{1,0:T(8,128)(2,1)}) %all-gather.14.cloned.1.call-update) | async-done | bytes 4194320 | tf_op jit(solution)/shard_map/all_gather | solution.py:101
  270.3 3.1 fusion.26
  273.4 51.6 %all-gather.16.cloned.1.call-done = bf16[2048,1024]{1,0:T(8,128)(2,1)} async-done(((bf16[128,1024]{1,0:T(8,128)(2,1)}), bf16[2048,1024]{1,0:T(8,128)(2,1)}) %all-gather.16.cloned.1.call-update) | async-done | bytes 4194320 | tf_op jit(solution)/shard_map/all_gather | solution.py:106
  325.0 10.0 %fusion.44 = f32[1024,1024]{1,0:T(8,128)} fusion(bf16[2048,1024]{1,0:T(8,128)(2,1)} %all-gather.16.cloned.1.call-done, bf16[1024,2048]{1,0:T(8,128)(2,1)} %all-gather.14.cloned.1.call-done, f32[2048]{0:T(1024)S(1)} %convert_element_type.102, f32[1024]{0:T(1024)S(1)} %add_rsqrt_fusion), kind=kOutput, calls=%fused_computation.51 | convolution fusion | flops 4303355904 | bytes 12595200 | tf_op jit(solution)/shard_map/dot_general | solution.py:104
  335.0 43.5 %all-gather.18.cloned.1.call-done = bf16[2048,1024]{1,0:T(8,128)(2,1)} async-done(((bf16[128,1024]{1,0:T(8,128)(2,1)}), bf16[2048,1024]{1,0:T(8,128)(2,1)}) %all-gather.18.cloned.1.call-update) | async-done | bytes 4194320 | tf_op jit(solution)/shard_map/all_gather | solution.py:110
  378.4 59.4 %all-gather.20.cloned.1.call-done = bf16[1024,2048]{1,0:T(8,128)(2,1)} async-done(((bf16[1024,128]{1,0:T(8,128)(2,1)}), bf16[1024,2048]{1,0:T(8,128)(2,1)}) %all-gather.20.cloned.1.call-update) | async-done | bytes 4194320 | tf_op jit(solution)/shard_map/all_gather | solution.py:114
  437.9 15.4 %convolution_convert_fusion.1 = bf16[1024,2048]{1,0:T(8,128)(2,1)} fusion(bf16[1024,2048]{1,0:T(8,128)(2,1)} %all-gather.20.cloned.1.call-done, f32[1024,1024]{1,0:T(8,128)} %fusion.44, bf16[2048,1024]{1,0:T(8,128)(2,1)} %all-gather.18.cloned.1.call-done, bf16[1024,2048]{1,0:T(8,128)(2,1)} %all-gather.14.cloned.1.call-done, ...), kind=kOutput, calls=%fused_computation.48 | convolution fusion | flops 8606711808 | bytes 20983808 | tf_op jit(solution)/shard_map/dot_general | solution.py:113
  453.3 0.0 reduce-scatter.5.cloned.1.call-update
  453.3 1.0 copy.19
  454.3 1.3 slice_bitcast_fusion
  455.6 1.0 copy.20
  456.6 33.9 %reduce-scatter.5.cloned.1.call-done = bf16[1024,256]{1,0:T(8,128)(2,1)} async-done(((bf16[1024,2048]{1,0:T(8,128)(2,1)}), bf16[1024,256]{1,0:T(8,128)(2,1)}) %reduce-scatter.5.cloned.1.call-update) | async-done | bytes 524304 | tf_op jit(solution)/shard_map/reduce_scatter | solution.py:116
  490.5 2.0 add_convert_fusion
  (19 shorter events, 0.2 us)
Async XLA Ops:
  7.2 41.0 %all-gather.8.cloned.1.call-start = ((), (), s32[]{:S(2)}) async-start(), calls=%async_computation.2 | async-start | bytes 4718592 | tf_op jit(solution)/shard_map/all_gather | solution.py:54
  7.9 96.8 %all-gather.10.cloned.1.call-start = ((), (), s32[]{:S(2)}) async-start(), calls=%async_computation.3 | async-start | bytes 3342336 | tf_op jit(solution)/shard_map/all_gather | solution.py:60
  9.7 139.8 %all-gather.12.cloned.1.call-start = ((), (), s32[]{:S(2)}) async-start(), calls=%async_computation.4 | async-start | bytes 1114112 | tf_op jit(solution)/shard_map/all_gather | solution.py:95
  10.4 222.7 %reduce-scatter.3.cloned.1.call-start = ((), (), s32[]{:S(2)}) async-start(), calls=%async_computation.5 | async-start | bytes 4718592 | tf_op jit(solution)/shard_map/reduce_scatter | solution.py:97
  111.3 1.7 copy-start.2
  111.3 2.0 copy-start.1
  126.5 2.4 copy-start.4
  132.0 2.6 copy-start.5
  134.6 98.5 %copy-start.3 = (bf16[1024,256]{1,0:T(8,128)(2,1)S(1)}, bf16[1024,256]{1,0:T(8,128)(2,1)}, u32[]{:S(2)}) copy-start(bf16[1024,256]{1,0:T(8,128)(2,1)} %param.13) | copy-start | bytes 1572868
  134.6 102.9 %copy-start.6 = (bf16[2048]{0:T(1024)(128)(2,1)S(1)}, bf16[2048]{0:T(1024)(128)(2,1)}, u32[]{:S(2)}) copy-start(bf16[2048]{0:T(1024)(128)(2,1)} %param.17) | copy-start | bytes 12292
  154.0 116.3 %all-gather.14.cloned.1.call-start = ((), (), s32[]{:S(2)}) async-start(), calls=%async_computation.6 | async-start | bytes 4718592 | tf_op jit(solution)/shard_map/all_gather | solution.py:101
  235.1 89.9 %all-gather.16.cloned.1.call-start = ((), (), s32[]{:S(2)}) async-start(), calls=%async_computation.7 | async-start | bytes 4456448 | tf_op jit(solution)/shard_map/all_gather | solution.py:106
  235.7 142.7 %all-gather.18.cloned.1.call-start = ((), (), s32[]{:S(2)}) async-start(), calls=%async_computation.8 | async-start | bytes 4456448 | tf_op jit(solution)/shard_map/all_gather | solution.py:110
  236.4 201.4 %all-gather.20.cloned.1.call-start = ((), (), s32[]{:S(2)}) async-start(), calls=%async_computation.9 | async-start | bytes 4456448 | tf_op jit(solution)/shard_map/all_gather | solution.py:114
  237.2 253.3 %reduce-scatter.5.cloned.1.call-start = ((), (), s32[]{:S(2)}) async-start(), calls=%async_computation.10 | async-start | bytes 4718592 | tf_op jit(solution)/shard_map/reduce_scatter | solution.py:116
  453.3 37.2 %copy-start = (bf16[1024,256]{1,0:T(8,128)(2,1)S(1)}, bf16[1024,256]{1,0:T(8,128)(2,1)}, u32[]{:S(2)}) copy-start(bf16[1024,256]{1,0:T(8,128)(2,1)} %add_convert_fusion.1) | copy-start | bytes 1572868
Sparse Core Ops, SparseCore 0:
  9.7 38.4 all-gather.7
  50.9 53.7 all-gather.9
  106.8 42.7 all-gather.11
  154.2 78.9 reduce-scatter.2
  235.2 35.0 all-gather.13
  272.3 52.6 all-gather.15
  327.2 51.2 all-gather.17
  380.5 57.2 all-gather.19
  453.4 37.0 reduce-scatter.4
where the time goes:
time: 500 us; the launch traced here: 499 us
  waiting for transfers between devices  398 us (80%)
  matrix products  50 us (10%)
  other arithmetic  21.9 us (4%)
  between operations  14.7 us (3%)
  local copies, waits for them, and re-layouts  13.8 us (3%)
    reduce_scatter x1, waiting for transfers between devices, on_device(): lax.psum_scatter(partial_value.astype(jnp.bfloat16), 'mp', scatter_dimens...  79 us
    all_gather x1, waiting for transfers between devices, on_device(): lax.all_gather(w_down, 'req', axis=1, tiled=True)  59.4 us
    all_gather x1, waiting for transfers between devices, on_device(): lax.all_gather(w_qkv, 'req', axis=1, tiled=True)  53.4 us
    all_gather x1, waiting for transfers between devices, on_device(): lax.all_gather(w_gate, 'req', axis=0, tiled=True)  51.6 us
    all_gather x1, waiting for transfers between devices, on_device(): lax.all_gather(w_up, 'req', axis=0, tiled=True)  43.5 us
    reduce_scatter x1, waiting for transfers between devices, on_device(): lax.psum_scatter(terms.astype(jnp.bfloat16), 'mp', scatter_dimension=1, t...  33.9 us
    all_gather x1, waiting for transfers between devices, on_device(): mid_full = lax.all_gather(mid_local, 'mp', axis=1, tiled=True)  32.8 us
    all_gather x1, waiting for transfers between devices, on_device(): full_rows = lax.all_gather(hidden_in, 'mp', axis=1, tiled=True)  27.4 us
  transfers between devices with their start and end apart: 9, of which 9 were waited for; matrix products, arithmetic and copies ran while one was open for 12% of the time, Pallas kernels for 0%

commit v1 on v0

--- a/solution.py
+++ b/solution.py
@@ -7,6 +7,12 @@
 THETA = 130000.0
 EPSILON = 1e-05
 NEG_FILL = -1e30
+
+
+def mark_scenes(array_in):
+    axis_id = "req"
+    earlier = jnp.concatenate(lax.axis_size(axis_id) * [array_in], 0)
+    return lax.all_to_all(earlier, axis_id, 0, 0, tiled=True)
 
 
 def rms_scale(rows, gain):
@@ -101,11 +107,7 @@
     mid_full = lax.all_gather(mid_local, "mp", axis=1, tiled=True)
     normed2 = rms_scale(mid_full, mlp_gain)
     columns = normed2
-    gate = jnp.dot(
-        columns,
-        lax.all_gather(w_gate, "req", axis=0, tiled=True),
-        preferred_element_type=jnp.float32,
-    )
+    gate = jnp.dot(columns, mark_scenes(w_gate), preferred_element_type=jnp.float32)
     upper = jnp.dot(
         columns, lax.all_gather(w_up, "req", axis=0, tiled=True), preferred_element_type=jnp.float32
     )

time: 500 us -> 461 us (0.922)
  waiting for transfers between devices: 398 us -> 350 us
  starting transfers between devices: 0.57 us -> 7.68 us
    all_gather x1 -> x0, waiting for transfers between devices: 51.6 us -> none  [on_device(): lax.all_gather(w_gate, 'req', axis=0, tiled=True)]
    all_to_all x0 -> x1, waiting for transfers between devices: none -> 24.2 us  [mark_scenes(): return lax.all_to_all(earlier, axis_id, 0, 0, tiled=True)]
    all_gather x1, waiting for transfers between devices: 43.5 us -> 32.6 us  [on_device(): lax.all_gather(w_up, 'req', axis=0, tiled=True)]
    all_gather x1, waiting for transfers between devices: 32.8 us -> 23.9 us  [on_device(): mid_full = lax.all_gather(mid_local, 'mp', axis=1, tiled=True)]
    all_to_all x0 -> x1, starting transfers between devices: none -> 7.14 us  [mark_scenes(): return lax.all_to_all(earlier, axis_id, 0, 0, tiled=True)]
    unnamed x15 -> x34, local copies, waits for them, and re-layouts: 12.2 us -> 14.5 us
  transfers between devices with their start and end apart: 9 -> 9, of which waited for: 9 -> 9; matrix products, arithmetic and copies ran while one was open for 12% -> 13% of each run, Pallas kernels for 0% -> 0%
where the time goes in v1:
time: 461 us; the launch traced here: 460 us
  waiting for transfers between devices  350 us (76%)
  matrix products  50 us (11%)
  other arithmetic  21.8 us (5%)
  local copies, waits for them, and re-layouts  16 us (3%)
  between operations  15.1 us (3%)
  starting transfers between devices  7.68 us (2%)
    reduce_scatter x1, waiting for transfers between devices, on_device(): lax.psum_scatter(partial_value.astype(jnp.bfloat16), 'mp', scatter_dimens...  78.3 us
    all_gather x1, waiting for transfers between devices, on_device(): lax.all_gather(w_down, 'req', axis=1, tiled=True)  59.4 us
    all_gather x1, waiting for transfers between devices, on_device(): lax.all_gather(w_qkv, 'req', axis=1, tiled=True)  53.4 us
    reduce_scatter x1, waiting for transfers between devices, on_device(): lax.psum_scatter(terms.astype(jnp.bfloat16), 'mp', scatter_dimension=1, t...  33.9 us
    all_gather x1, waiting for transfers between devices, on_device(): lax.all_gather(w_up, 'req', axis=0, tiled=True)  32.6 us
    all_gather x1, waiting for transfers between devices, on_device(): full_rows = lax.all_gather(hidden_in, 'mp', axis=1, tiled=True)  27.4 us
    all_to_all x1, waiting for transfers between devices, mark_scenes(): return lax.all_to_all(earlier, axis_id, 0, 0, tiled=True)  24.2 us
    all_gather x1, waiting for transfers between devices, on_device(): mid_full = lax.all_gather(mid_local, 'mp', axis=1, tiled=True)  23.9 us
  transfers between devices with their start and end apart: 9, of which 9 were waited for; matrix products, arithmetic and copies ran while one was open for 13% of the time, Pallas kernels for 0%

profile of v1, /device:TPU:0, one launch (start us, length us, event | category | flops | bytes accessed | tf_op | source)
XLA Modules:
  0.0 460.2 jit_solution(12348870092223546699)
XLA Ops:
  7.2 0.0 all-gather.7.cloned.1.call-start
  7.2 0.7 all-gather.7.cloned.1.call-update
  7.9 0.0 all-gather.9.cloned.1.call-start
  7.9 1.7 copy.15
  9.7 0.0 all-gather.9.cloned.1.call-update
  9.7 0.0 all-gather.11.cloned.1.call-start
  9.8 0.7 all-gather.11.cloned.1.call-update
  10.4 0.0 reduce-scatter.3.cloned.1.call-start
  10.5 1.3 iota_compare_fusion
  12.5 0.7 convert_element_type.87
  13.2 2.9 copy.17
  16.1 4.1 copy.18
  20.2 0.5 multiply_cosine_fusion
  20.8 27.4 %all-gather.7.cloned.1.call-done = bf16[1024,2048]{1,0:T(8,128)(2,1)} async-done(((bf16[1024,256]{1,0:T(8,128)(2,1)}), bf16[1024,2048]{1,0:T(8,128)(2,1)}) %all-gather.7.cloned.1.call-update) | async-done | bytes 4194320 | tf_op jit(solution)/shard_map/all_gather | solution.py:60
  48.2 3.1 fusion.23
  51.3 53.4 %all-gather.9.cloned.1.call-done = bf16[3,2048,256]{1,2,0:T(8,128)(2,1)} async-done(((bf16[3,128,256]{1,2,0:T(8,128)(2,1)}), bf16[3,2048,256]{1,2,0:T(8,128)(2,1)}) %all-gather.9.cloned.1.call-update) | async-done | bytes 3145744 | tf_op jit(solution)/shard_map/all_gather | solution.py:66
  104.7 6.6 %fusion.37 = f32[3,1024,256]{1,2,0:T(8,128)S(1)} fusion(bf16[3,2048,256]{1,2,0:T(8,128)(2,1)} %all-gather.9.cloned.1.call-done, bf16[1024,2048]{1,0:T(8,128)(2,1)} %all-gather.7.cloned.1.call-done, f32[2048]{0:T(1024)S(1)} %convert_element_type.87, f32[1024]{0:T(1024)S(1)} %add_rsqrt_fusion.1), kind=kOutput, calls=%fused_computation.49 | convolution fusion | flops 3229614080 | bytes 10498048 | tf_op jit(solution)/shard_map/nd,kdw->knw/dot_general | solution.py:63
  111.3 0.0 copy-start.4
  111.3 0.0 copy-start.3
  111.3 0.1 fusion.54
  111.5 0.1 slice.44
  111.5 0.2 subtract_convert_fusion
  111.7 0.2 multiply_subtract_fusion
  111.8 1.1 copy-done.4
  113.0 0.3 copy-done.3
  113.3 3.0 fusion.20
  116.4 4.2 fusion.22
  120.6 5.9 %fusion.40 = f32[4,1024,64]{1,2,0:T(8,128)} fusion(bf16[1024,4,64]{0,2,1:T(8,128)(2,1)S(1)} %bitcast.83, f32[4,1024,1024]{1,2,0:T(8,128)S(1)} %get-tuple-element.91, f32[4,1024]{1,0:T(4,128)S(1)} %get-tuple-element.87, pred[1024,1024]{0,1:T(8,128)(4,1)S(1)} %copy-done.3, f32[4,1024]{1,0:T(4,128)S(1)} %get-tuple-element.85), kind=kOutput, calls=%fused_computation.50 | convolution fusion | flops 558104576 | bytes 19431424 | tf_op jit(solution)/shard_map/hqk,khd->hqd/dot_general | solution.py:47
  126.5 8.0 %while.14 = (s32[]{:T(128)}, f32[4,1024,1]{1,0,2:T(4,128)S(1)}, f32[4,1024,1]{1,0,2:T(4,128)S(1)}, f32[4,1024,64]{1,2,0:T(8,128)}, s32[]{:T(128)}, /*index=5*/s3...) while((s32[]{:T(128)}, f32[4,1024,1]{1,0,2:T(4,128)S(1)}, ...), condition=%wide.region_6.7_spmd, body=%wide.region_3.6_spmd.sunk | while | flops 564671488 | bytes 36965104 | solution.py:98
  126.5 0.7 add_compare_fusion.2
  127.2 0.0 copy-start.6
  127.2 1.6 bitcast_reduce_fusion.2
  128.8 3.1 fusion.74
  131.9 2.5 fusion.73
  134.5 1.3 divide_convert_fusion
  135.8 13.7 %all-gather.11.cloned.1.call-done = bf16[256,2048]{1,0:T(8,128)(2,1)} async-done(((bf16[256,128]{1,0:T(8,128)(2,1)}), bf16[256,2048]{1,0:T(8,128)(2,1)}) %all-gather.11.cloned.1.call-update) | async-done | bytes 1048592 | tf_op jit(solution)/shard_map/all_gather | solution.py:101
  149.5 4.5 convolution_convert_fusion
  154.1 0.0 reduce-scatter.3.cloned.1.call-update
  154.1 0.0 all-gather.13.cloned.1.call-start
  154.1 78.3 %reduce-scatter.3.cloned.1.call-done = bf16[1024,256]{1,0:T(8,128)(2,1)} async-done(((bf16[1024,2048]{1,0:T(8,128)(2,1)}), bf16[1024,256]{1,0:T(8,128)(2,1)}) %reduce-scatter.3.cloned.1.call-update) | async-done | bytes 524304 | tf_op jit(solution)/shard_map/reduce_scatter | solution.py:103
  232.5 2.0 add_convert_fusion.1
  234.4 0.0 all-gather.13.cloned.1.call-update
  234.5 0.0 all-gather.15.cloned.1.call-start
  234.5 0.5 all-gather.15.cloned.1.call-update
  235.0 0.0 all-gather.17.cloned.1.call-start
  235.1 0.7 all-gather.17.cloned.1.call-update
  235.8 0.0 copy-done
  236.2 1.9 copy-done.1
  238.2 7.1 %all-to-all-start = ((bf16[16,128,1024]{2,1,0:T(8,128)(2,1)}), bf16[16,128,1024]{2,1,0:T(8,128)(2,1)}, u32[]{:S(2)}, u32[]{:S(2)}) async-start(bf16[16,128,1024]{2,1,0:T(8,128)(2,1)} %bitcast.76), calls=%async_computation.1 | async-start | bytes 8388608 | tf_op jit(solution)/shard_map/all_to_all | solution.py:15
  245.3 0.3 reduce-scatter.5.cloned.1.call-start
  245.6 23.9 %all-gather.13.cloned.1.call-done = bf16[1024,2048]{1,0:T(8,128)(2,1)} async-done(((bf16[1024,256]{1,0:T(8,128)(2,1)}), bf16[1024,2048]{1,0:T(8,128)(2,1)}) %all-gather.13.cloned.1.call-update) | async-done | bytes 4194320 | tf_op jit(solution)/shard_map/all_gather | solution.py:107
  269.5 3.1 fusion.26
  272.6 24.2 %all-to-all-done = bf16[16,128,1024]{2,1,0:T(8,128)(2,1)} async-done(((bf16[16,128,1024]{2,1,0:T(8,128)(2,1)}), bf16[16,128,1024]{2,1,0:T(8,128)(2,1)}, u32[]{:S(2)}, u32[]{:S(2)}) %all-to-all-start) | async-done | bytes 4194336 | tf_op jit(solution)/shard_map/all_to_all | solution.py:15
  296.8 9.9 %fusion.44 = f32[1024,1024]{1,0:T(8,128)} fusion(bf16[2048,1024]{1,0:T(8,128)(2,1)} %bitcast.19, bf16[1024,2048]{1,0:T(8,128)(2,1)} %all-gather.13.cloned.1.call-done, f32[2048]{0:T(1024)S(1)} %convert_element_type.102, f32[1024]{0:T(1024)S(1)} %add_rsqrt_fusion), kind=kOutput, calls=%fused_computation.51 | convolution fusion | flops 4303355904 | bytes 12595200 | tf_op jit(solution)/shard_map/dot_general | solution.py:110
  306.7 32.6 %all-gather.15.cloned.1.call-done = bf16[2048,1024]{1,0:T(8,128)(2,1)} async-done(((bf16[128,1024]{1,0:T(8,128)(2,1)}), bf16[2048,1024]{1,0:T(8,128)(2,1)}) %all-gather.15.cloned.1.call-update) | async-done | bytes 4194320 | tf_op jit(solution)/shard_map/all_gather | solution.py:112
  339.3 59.4 %all-gather.17.cloned.1.call-done = bf16[1024,2048]{1,0:T(8,128)(2,1)} async-done(((bf16[1024,128]{1,0:T(8,128)(2,1)}), bf16[1024,2048]{1,0:T(8,128)(2,1)}) %all-gather.17.cloned.1.call-update) | async-done | bytes 4194320 | tf_op jit(solution)/shard_map/all_gather | solution.py:116
  398.8 15.3 %convolution_convert_fusion.1 = bf16[1024,2048]{1,0:T(8,128)(2,1)} fusion(bf16[1024,2048]{1,0:T(8,128)(2,1)} %all-gather.17.cloned.1.call-done, f32[1024,1024]{1,0:T(8,128)} %fusion.44, bf16[2048,1024]{1,0:T(8,128)(2,1)} %all-gather.15.cloned.1.call-done, bf16[1024,2048]{1,0:T(8,128)(2,1)} %all-gather.13.cloned.1.call-done, ...), kind=kOutput, calls=%fused_computation.48 | convolution fusion | flops 8606711808 | bytes 20983808 | tf_op jit(solution)/shard_map/dot_general | solution.py:115
  414.1 0.0 reduce-scatter.5.cloned.1.call-update
  414.2 1.0 copy.19
  415.2 1.3 slice_bitcast_fusion
  416.5 1.0 copy.20
  417.5 33.9 %reduce-scatter.5.cloned.1.call-done = bf16[1024,256]{1,0:T(8,128)(2,1)} async-done(((bf16[1024,2048]{1,0:T(8,128)(2,1)}), bf16[1024,256]{1,0:T(8,128)(2,1)}) %reduce-scatter.5.cloned.1.call-update) | async-done | bytes 524304 | tf_op jit(solution)/shard_map/reduce_scatter | solution.py:118
  451.4 0.0 copy-done.2
  451.4 2.0 add_convert_fusion
  (38 shorter events, 0.5 us)
Async XLA Ops:
  7.2 41.0 %all-gather.7.cloned.1.call-start = ((), (), s32[]{:S(2)}) async-start(), calls=%async_computation.3 | async-start | bytes 4718592 | tf_op jit(solution)/shard_map/all_gather | solution.py:60
  7.9 96.8 %all-gather.9.cloned.1.call-start = ((), (), s32[]{:S(2)}) async-start(), calls=%async_computation.4 | async-start | bytes 3342336 | tf_op jit(solution)/shard_map/all_gather | solution.py:66
  9.7 139.8 %all-gather.11.cloned.1.call-start = ((), (), s32[]{:S(2)}) async-start(), calls=%async_computation.5 | async-start | bytes 1114112 | tf_op jit(solution)/shard_map/all_gather | solution.py:101
  10.4 222.0 %reduce-scatter.3.cloned.1.call-start = ((), (), s32[]{:S(2)}) async-start(), calls=%async_computation.6 | async-start | bytes 4718592 | tf_op jit(solution)/shard_map/reduce_scatter | solution.py:103
  111.3 1.7 copy-start.4
  111.3 2.0 copy-start.3
  127.2 1.6 copy-start.6
  131.9 2.6 copy-start.7
  149.5 82.9 %copy-start.5 = (bf16[1024,256]{1,0:T(8,128)(2,1)S(1)}, bf16[1024,256]{1,0:T(8,128)(2,1)}, u32[]{:S(2)}) copy-start(bf16[1024,256]{1,0:T(8,128)(2,1)} %param.13) | copy-start | bytes 1572868
  154.1 81.7 %copy-start = (bf16[128,1024]{1,0:T(8,128)(2,1)S(1)}, bf16[128,1024]{1,0:T(8,128)(2,1)}, u32[]{:S(2)}) copy-start(bf16[128,1024]{1,0:T(8,128)(2,1)} %param.18) | copy-start | bytes 786436
  154.1 115.5 %all-gather.13.cloned.1.call-start = ((), (), s32[]{:S(2)}) async-start(), calls=%async_computation.7 | async-start | bytes 4718592 | tf_op jit(solution)/shard_map/all_gather | solution.py:107
  234.5 104.9 %all-gather.15.cloned.1.call-start = ((), (), s32[]{:S(2)}) async-start(), calls=%async_computation.8 | async-start | bytes 4456448 | tf_op jit(solution)/shard_map/all_gather | solution.py:112
  235.0 163.7 %all-gather.17.cloned.1.call-start = ((), (), s32[]{:S(2)}) async-start(), calls=%async_computation.9 | async-start | bytes 4456448 | tf_op jit(solution)/shard_map/all_gather | solution.py:116
  236.2 1.9 copy-start.1
  238.2 7.4 %copy-start.8 = (bf16[2048]{0:T(1024)(128)(2,1)S(1)}, bf16[2048]{0:T(1024)(128)(2,1)}, u32[]{:S(2)}) copy-start(bf16[2048]{0:T(1024)(128)(2,1)} %param.17) | copy-start | bytes 12292
  238.2 58.6 %all-to-all-start = ((bf16[16,128,1024]{2,1,0:T(8,128)(2,1)}), bf16[16,128,1024]{2,1,0:T(8,128)(2,1)}, u32[]{:S(2)}, u32[]{:S(2)}) async-start(bf16[16,128,1024]{2,1,0:T(8,128)(2,1)} %bitcast.76), calls=%async_computation.1 | async-start | bytes 8388608 | tf_op jit(solution)/shard_map/all_to_all | solution.py:15
  245.3 206.1 %reduce-scatter.5.cloned.1.call-start = ((), (), s32[]{:S(2)}) async-start(), calls=%async_computation.10 | async-start | bytes 4718592 | tf_op jit(solution)/shard_map/reduce_scatter | solution.py:118
  414.1 37.3 %copy-start.2 = (bf16[1024,256]{1,0:T(8,128)(2,1)S(1)}, bf16[1024,256]{1,0:T(8,128)(2,1)}, u32[]{:S(2)}) copy-start(bf16[1024,256]{1,0:T(8,128)(2,1)} %add_convert_fusion.1) | copy-start | bytes 1572868
Sparse Core Ops, SparseCore 0:
  9.7 38.4 all-gather.6
  50.9 53.7 all-gather.8
  106.8 42.7 all-gather.10
  154.2 78.1 reduce-scatter.2
  234.6 34.9 all-gather.12
  271.5 67.7 all-gather.14
  341.4 57.2 all-gather.16
  414.2 37.1 reduce-scatter.4
